TPU v7x, 256 devices: a whole 4x4x8 slice. The times are simulated.
256 devices in a mesh: row: 16 (over z, core), col: 16 (over x, y).
Axes of the slice: x: 4, y: 4, z: 8, core: 2. Of those that a mesh axis runs over, the one named last changes fastest.
Arguments:
- site_tensor: bfloat16 [1024, 4, 1024], P('row', None, 'col'), may hold values from -180 to 180
- site_tangent: bfloat16 [1024, 4, 1024], P('row', None, 'col'), may hold values from -180 to 180
- left_env: bfloat16 [1024, 16384], P('row', 'col'), may hold values from -0.1875 to 0.375
- right_env: bfloat16 [1024, 16384], P('row', 'col'), may hold values from -0.046875 to 0.09375
- mpo: bfloat16 [16, 16, 4, 4], replicated, may hold values from -0.25 to 0.75
- dissipation: float32 [4], replicated, may hold values from 0.2 to 2
Outputs:
- evolved: float32 [1024, 4, 1024], P('row', None, 'col')
- evolved_tangent: float32 [1024, 4, 1024], P('row', None, 'col')
All inputs are finite; a program needn't handle non-finite values.
Results may differ from a plain program's by a relative error of at most 0.0055.
Values may be sent and summed in bfloat16 or wider, within the bound.
No kernel may reach another device: no remote copies, remote signals or barrier semaphores. Data moves between devices by JAX's collectives and lax.ppermute only.
A program may use at most 64 MiB of HBM per device.

v0:
```python
import jax
import jax.numpy as jnp
from jax import lax
from jax.sharding import PartitionSpec as P

KRYLOV = 3
taylor_order = 16


def inner(first, second):
    return jnp.sum(first * second)


def total(values):
    return lax.psum(lax.psum(values, "col"), "row")


def taylor(hess, dhess):
    size = hess.shape[0]
    term = jnp.zeros((size,), jnp.float32).at[0].set(1.0)
    dterm = jnp.zeros((size,), jnp.float32)
    total = term
    dtotal = dterm
    for order in range(1, taylor_order + 1):
        nterm = jnp.dot(hess, term, precision=lax.Precision.HIGHEST) / order
        dterm = (
            jnp.dot(dhess, term, precision=lax.Precision.HIGHEST)
            + jnp.dot(hess, dterm, precision=lax.Precision.HIGHEST)
        ) / order
        term = nterm
        total = total + term
        dtotal = dtotal + dterm
    return (total, dtotal)


def local(site_tensor, site_tangent, left_env, right_env, mpo, dissipation):
    rows_here, physical, cols_here = site_tensor.shape
    channels = mpo.shape[0]
    left_whole = lax.all_gather(left_env, "col", axis=1, tiled=True)
    right_whole = lax.all_gather(right_env, "row", axis=0, tiled=True)

    def apply(stacked):
        panels = stacked.shape[1]
        whole = lax.all_gather(stacked.astype(jnp.bfloat16), "row", axis=0, tiled=True)
        flat = whole.reshape(whole.shape[0], panels * physical * cols_here)
        left_three = left_whole.reshape(rows_here, flat.shape[0], channels)
        mixed = lax.dot_general(
            left_three, flat, (((1,), (0,)), ((), ())), preferred_element_type=jnp.float32
        )
        mixed = mixed.astype(jnp.bfloat16).reshape(rows_here, channels, panels, physical, cols_here)
        channel = jnp.einsum("awspr,wvpq->asqrv", mixed, mpo, preferred_element_type=jnp.float32)
        channel = channel.astype(jnp.bfloat16).reshape(
            rows_here * panels * physical, cols_here * channels
        )
        partial_rows = lax.dot_general(
            channel, right_whole, (((1,), (1,)), ((), ())), preferred_element_type=jnp.float32
        )
        partial_rows = partial_rows.reshape(rows_here, panels, physical, partial_rows.shape[1])
        summed = lax.psum_scatter(partial_rows, "col", scatter_dimension=3, tiled=True)
        return summed - dissipation[None, None, :, None] * stacked

    primal = site_tensor.astype(jnp.float32)
    tangent = site_tangent.astype(jnp.float32)
    starting = total(jnp.stack([inner(primal, primal), inner(primal, tangent)]))
    norm_site = jnp.sqrt(starting[0])
    norm_tangent = starting[1] / norm_site
    basis = [primal / norm_site]
    tangents = [(tangent - basis[0] * norm_tangent) / norm_site]
    hess = jnp.zeros((KRYLOV, KRYLOV), jnp.float32)
    dhess = jnp.zeros((KRYLOV, KRYLOV), jnp.float32)
    gram = jnp.zeros((KRYLOV, KRYLOV), jnp.float32)
    cross = jnp.zeros((KRYLOV, KRYLOV), jnp.float32)
    for level in range(KRYLOV):
        both = apply(jnp.stack([basis[level], tangents[level]], axis=1))
        image = both[:, 0]
        dimage = both[:, 1]
        counted = level + 1
        locals_list = [inner(vector, image) for vector in basis]
        locals_list = locals_list + [inner(vector, image) for vector in tangents]
        locals_list = locals_list + [inner(vector, dimage) for vector in basis]
        last = level + 1 == KRYLOV
        if not last:
            newest = basis[level]
            locals_list = locals_list + [inner(image, image), inner(image, dimage)]
            locals_list = locals_list + [inner(newest, vector) for vector in basis]
            locals_list = locals_list + [inner(newest, vector) for vector in tangents]
            locals_list = locals_list + [inner(vector, tangents[level]) for vector in basis[:level]]
        totals = total(jnp.stack(locals_list))
        coeffs = totals[:counted]
        across = totals[counted : 2 * counted]
        along = totals[2 * counted : 3 * counted]
        dcoeffs = across + along
        hess = hess.at[:counted, level].set(coeffs)
        dhess = dhess.at[:counted, level].set(dcoeffs)
        if not last:
            at = 3 * counted
            squared_image = totals[at]
            image_dimage = totals[at + 1]
            at += 2
            gram = gram.at[level, :counted].set(totals[at : at + counted])
            gram = gram.at[:counted, level].set(totals[at : at + counted])
            at += counted
            cross = cross.at[level, :counted].set(totals[at : at + counted])
            at += counted
            cross = cross.at[:level, level].set(totals[at : at + level])
            g = gram[:counted, :counted]
            t = cross[:counted, :counted]
            squared = (
                squared_image
                - 2.0 * jnp.sum(coeffs * coeffs)
                + jnp.dot(
                    coeffs,
                    jnp.dot(g, coeffs, precision=lax.Precision.HIGHEST),
                    precision=lax.Precision.HIGHEST,
                )
            )
            mixed_term = (
                image_dimage
                - jnp.sum(dcoeffs * coeffs)
                - jnp.sum(coeffs * across)
                - jnp.sum(coeffs * along)
                + jnp.dot(
                    coeffs,
                    jnp.dot(g, dcoeffs, precision=lax.Precision.HIGHEST),
                    precision=lax.Precision.HIGHEST,
                )
                + jnp.dot(
                    coeffs,
                    jnp.dot(t, coeffs, precision=lax.Precision.HIGHEST),
                    precision=lax.Precision.HIGHEST,
                )
            )
            residual = image
            dresidual = dimage
            for index in range(counted):
                residual = residual - coeffs[index] * basis[index]
                dresidual = (
                    dresidual - dcoeffs[index] * basis[index] - coeffs[index] * tangents[index]
                )
            height = jnp.sqrt(squared)
            dheight = mixed_term / height
            newvec = residual / height
            basis.append(newvec)
            tangents.append((dresidual - newvec * dheight) / height)
            hess = hess.at[level + 1, level].set(height)
            dhess = dhess.at[level + 1, level].set(dheight)
    coeff, dcoeff = taylor(hess, dhess)
    spread = jnp.zeros_like(primal)
    dspread = jnp.zeros_like(primal)
    for index in range(KRYLOV):
        spread = spread + coeff[index] * basis[index]
        dspread = dspread + coeff[index] * tangents[index] + dcoeff[index] * basis[index]
    evolved = norm_site * spread
    evolved_tangent = norm_tangent * spread + norm_site * dspread
    return (evolved, evolved_tangent)


def solution(mesh):
    in_specs = (
        P("row", None, "col"),
        P("row", None, "col"),
        P("row", "col"),
        P("row", "col"),
        P(),
        P(),
    )
    out_specs = (P("row", None, "col"), P("row", None, "col"))
    return jax.shard_map(local, mesh=mesh, in_specs=in_specs, out_specs=out_specs, check_vma=False)
```

profile of v0, /device:TPU:1, one launch (start us, length us, event | category | flops | bytes accessed | tf_op | source)
XLA Modules:
  0.0 870.2 jit_solution(10881828648179970118)
XLA Ops:
  7.2 1.5 fusion.79
  8.7 1.4 pad_maximum_fusion.3
  10.1 34.2 %psum.56 = f32[2]{0:T(128)S(1)} all-reduce(f32[2]{0:T(128)S(1)} %pad_maximum_fusion.3), channel_id=1, replica_groups=mesh['row'=16,'col'=16] {'col'}, use_global_device_ids=true, to_apply=%region_2.0 | all-reduce | flops 2 | bytes 16 | tf_op jit(solution)/shard_map/psum | solution.py:15
  44.3 33.8 %psum.57 = f32[2]{0:T(128)S(1)} all-reduce(f32[2]{0:T(128)S(1)} %psum.56), channel_id=1, replica_groups=mesh['row'=16,'col'=16] {'row'}, use_global_device_ids=true, to_apply=%region_3.0 | all-reduce | flops 2 | bytes 16 | tf_op jit(solution)/shard_map/psum | solution.py:15
  80.1 0.9 fusion.138
  83.3 1.0 copy.138
  84.3 32.3 %all-gather.6.cloned.1.call-done = bf16[1024,2,4,64]{3,2,1,0:T(4,128)(2,1)} async-done(((bf16[64,2,4,64]{3,2,1,0:T(4,128)(2,1)}), bf16[1024,2,4,64]{3,2,1,0:T(4,128)(2,1)}) %all-gather.6.cloned.1.call-update) | async-done | bytes 1048592 | tf_op jit(solution)/shard_map/all_gather | solution.py:44
  116.6 4.1 copy.109
  120.7 44.7 %all-gather.8.cloned.1.call-done = bf16[64,16384]{1,0:T(8,128)(2,1)} async-done(((bf16[64,1024]{1,0:T(8,128)(2,1)}), bf16[64,16384]{1,0:T(8,128)(2,1)}) %all-gather.8.cloned.1.call-update) | async-done | bytes 2097168 | tf_op jit(solution)/shard_map/all_gather | solution.py:39
  165.5 4.8 copy.110
  170.2 4.5 copy.112
  174.7 3.5 fusion.18
  178.2 4.7 reshape.536
  182.9 4.7 fusion.9
  187.6 5.8 copy.115
  193.4 14.8 %all-gather.10.cloned.1.call-done = bf16[1024,1024]{1,0:T(8,128)(2,1)} async-done(((bf16[64,1024]{1,0:T(8,128)(2,1)}), bf16[1024,1024]{1,0:T(8,128)(2,1)}) %all-gather.10.cloned.1.call-update) | async-done | bytes 2097168 | tf_op jit(solution)/shard_map/all_gather | solution.py:40
  208.1 6.0 fusion.5
  214.1 4.8 copy.173
  218.9 5.6 reshape.685
  225.0 76.2 %reduce-scatter.10.cloned.1.call-done = f32[64,512]{1,0:T(8,128)} async-done(((f32[1024,512]{1,0:T(8,128)}), f32[64,512]{1,0:T(8,128)}) %reduce-scatter.10.cloned.1.call-update) | async-done | bytes 131088
  301.2 1.1 reshape.686
  302.6 0.8 multiply_reduce_fusion.24
  303.4 4.5 stack.145
  307.8 30.9 %psum.58 = f32[7]{0:T(128)S(1)} all-reduce(f32[7]{0:T(128)S(1)} %stack.145), channel_id=1, replica_groups=mesh['row'=16,'col'=16] {'col'}, use_global_device_ids=true, to_apply=%region_12.0 | all-reduce | flops 7 | bytes 56 | tf_op jit(solution)/shard_map/psum | solution.py:15
  338.7 32.9 %psum.59 = f32[7]{0:T(128)S(1)} all-reduce(f32[7]{0:T(128)S(1)} %psum.58), channel_id=1, replica_groups=mesh['row'=16,'col'=16] {'row'}, use_global_device_ids=true, to_apply=%region_13.0 | all-reduce | flops 7 | bytes 56 | tf_op jit(solution)/shard_map/psum | solution.py:15
  384.9 35.9 %all-gather.12.cloned.1.call-done = bf16[1024,2,4,64]{3,2,1,0:T(4,128)(2,1)} async-done(((bf16[64,2,4,64]{3,2,1,0:T(4,128)(2,1)}), bf16[1024,2,4,64]{3,2,1,0:T(4,128)(2,1)}) %all-gather.12.cloned.1.call-update) | async-done | bytes 1048592 | tf_op jit(solution)/shard_map/all_gather | solution.py:44
  420.8 4.1 copy.118
  424.9 3.5 fusion.19
  428.4 4.7 reshape.543
  433.1 4.7 fusion.12
  437.7 5.8 copy.123
  443.5 6.0 fusion.3
  449.5 4.8 copy.175
  454.3 5.6 reshape.687
  462.4 74.2 %reduce-scatter.12.cloned.1.call-done = f32[64,512]{1,0:T(8,128)} async-done(((f32[1024,512]{1,0:T(8,128)}), f32[64,512]{1,0:T(8,128)}) %reduce-scatter.12.cloned.1.call-update) | async-done | bytes 131088
  536.6 1.1 reshape.688
  538.0 0.9 multiply_reduce_fusion.14
  538.8 8.2 stack.162
  547.7 30.9 %psum.60 = f32[13]{0:T(128)S(1)} all-reduce(f32[13]{0:T(128)S(1)} %stack.162), channel_id=1, replica_groups=mesh['row'=16,'col'=16] {'col'}, use_global_device_ids=true, to_apply=%region_28.0 | all-reduce | flops 13 | bytes 104 | tf_op jit(solution)/shard_map/psum | solution.py:15
  578.6 33.1 %psum.61 = f32[13]{0:T(128)S(1)} all-reduce(f32[13]{0:T(128)S(1)} %psum.60), channel_id=1, replica_groups=mesh['row'=16,'col'=16] {'row'}, use_global_device_ids=true, to_apply=%region_29.0 | all-reduce | flops 13 | bytes 104 | tf_op jit(solution)/shard_map/psum | solution.py:15
  612.3 0.8 slice_bitcast_fusion.10
  613.3 1.5 scatter.70
  614.8 0.8 fusion.74
  617.0 1.8 dynamic-slice.126
  620.5 1.3 scatter.76
  628.2 2.7 subtract_divide_fusion
  631.7 35.9 %all-gather.14.cloned.1.call-done = bf16[1024,2,4,64]{3,2,1,0:T(4,128)(2,1)} async-done(((bf16[64,2,4,64]{3,2,1,0:T(4,128)(2,1)}), bf16[1024,2,4,64]{3,2,1,0:T(4,128)(2,1)}) %all-gather.14.cloned.1.call-update) | async-done | bytes 1048592 | tf_op jit(solution)/shard_map/all_gather | solution.py:44
  667.6 4.1 copy.127
  671.7 3.5 fusion.20
  675.2 3.5 reshape.554
  678.8 3.1 fusion.15
  681.8 5.8 copy.132
  687.6 4.6 fusion.1
  692.3 3.2 copy.177
  695.5 5.6 reshape.689
  702.2 1.4 scatter.64
  703.5 1.4 scatter.85
  704.9 73.0 %reduce-scatter.14.cloned.1.call-done = f32[64,512]{1,0:T(8,128)} async-done(((f32[1024,512]{1,0:T(8,128)}), f32[64,512]{1,0:T(8,128)}) %reduce-scatter.14.cloned.1.call-update) | async-done | bytes 131088
  777.9 1.1 reshape.690
  779.2 0.9 multiply_reduce_fusion
  780.0 5.7 stack.175
  785.9 30.9 %psum.62 = f32[9]{0:T(128)S(1)} all-reduce(f32[9]{0:T(128)S(1)} %stack.175), channel_id=1, replica_groups=mesh['row'=16,'col'=16] {'col'}, use_global_device_ids=true, to_apply=%region_45.0 | all-reduce | flops 9 | bytes 72 | tf_op jit(solution)/shard_map/psum | solution.py:15
  816.9 32.9 %psum.63 = f32[9]{0:T(128)S(1)} all-reduce(f32[9]{0:T(128)S(1)} %psum.62), channel_id=1, replica_groups=mesh['row'=16,'col'=16] {'row'}, use_global_device_ids=true, to_apply=%region_46.0 | all-reduce | flops 9 | bytes 72 | tf_op jit(solution)/shard_map/psum | solution.py:15
  857.8 3.9 multiply_add_fusion
  (114 shorter events, 24.1 us)
Async XLA Ops:
  7.2 109.4 %all-gather.6.cloned.1.call-start = ((), (), s32[]{:S(2)}) async-start(), calls=%async_computation.3 | async-start | bytes 2228224 | tf_op jit(solution)/shard_map/all_gather | solution.py:44
  81.8 83.7 %all-gather.8.cloned.1.call-start = ((), (), s32[]{:S(2)}) async-start(), calls=%async_computation.4 | async-start | bytes 2228224 | tf_op jit(solution)/shard_map/all_gather | solution.py:39
  82.5 125.6 %all-gather.10.cloned.1.call-start = ((), (), s32[]{:S(2)}) async-start(), calls=%async_computation.5 | async-start | bytes 2228224 | tf_op jit(solution)/shard_map/all_gather | solution.py:40
  83.3 218.0 %reduce-scatter.10.cloned.1.call-start = ((), (), s32[]{:S(2)}) async-start(), calls=%async_computation.8 | async-start | bytes 2228224
  224.5 78.0 %copy-start.2 = (f32[4]{0:T(128)S(1)}, f32[4]{0:T(128)}, u32[]{:S(2)}) copy-start(f32[4]{0:T(128)} %param.47) | copy-start | bytes 52
  224.5 78.1 %copy-start = (bf16[64,4,64]{2,1,0:T(4,128)(2,1)S(1)}, bf16[64,4,64]{2,1,0:T(4,128)(2,1)}, u32[]{:S(2)}) copy-start(bf16[64,4,64]{2,1,0:T(4,128)(2,1)} %param.42) | copy-start | bytes 98308
  224.5 78.1 %copy-start.1 = (bf16[64,4,64]{2,1,0:T(4,128)(2,1)S(1)}, bf16[64,4,64]{2,1,0:T(4,128)(2,1)}, u32[]{:S(2)}) copy-start(bf16[64,4,64]{2,1,0:T(4,128)(2,1)} %param.43) | copy-start | bytes 98308
  224.5 196.3 %all-gather.12.cloned.1.call-start = ((), (), s32[]{:S(2)}) async-start(), calls=%async_computation.6 | async-start | bytes 2228224 | tf_op jit(solution)/shard_map/all_gather | solution.py:44
  384.8 151.8 %reduce-scatter.12.cloned.1.call-start = ((), (), s32[]{:S(2)}) async-start(), calls=%async_computation.9 | async-start | bytes 2228224
  459.9 207.7 %all-gather.14.cloned.1.call-start = ((), (), s32[]{:S(2)}) async-start(), calls=%async_computation.7 | async-start | bytes 2228224 | tf_op jit(solution)/shard_map/all_gather | solution.py:44
  631.7 146.2 %reduce-scatter.14.cloned.1.call-start = ((), (), s32[]{:S(2)}) async-start(), calls=%async_computation.10 | async-start | bytes 2228224
  701.1 148.9 %copy-start.3 = (f32[3,1]{0,1:T(1,128)S(1)}, f32[3,1]{0,1:T(1,128)}, u32[]{:S(2)}) copy-start(f32[3,1]{0,1:T(1,128)} %constant.468) | copy-start | bytes 40
Sparse Core Ops, SparseCore 0:
  81.9 34.6 all-gather.5
  119.1 46.3 all-gather.7
  167.3 40.7 all-gather.9
  224.6 76.5 reduce-scatter.9
  385.0 35.7 all-gather.11
  460.0 76.5 reduce-scatter.11
  631.8 35.7 all-gather.13
  701.2 76.6 reduce-scatter.13
where the time goes:
time: 881 us; the launch traced here: 870 us
  waiting for transfers between devices  388 us (44%)
  blocking collectives  260 us (30%)
  local copies, waits for them, and re-layouts  123 us (14%)
  matrix products  48.2 us (5%)
  between operations  34.5 us (4%)
  other arithmetic  15.4 us (2%)
    psum x8, blocking collectives, total(): return lax.psum(lax.psum(values, 'col'), 'row')  260 us
    unnamed x11, waiting for transfers between devices  225 us
    all_gather x3, waiting for transfers between devices, apply(): lax.all_gather(stacked.astype(jnp.bfloat16), 'row', axis=0, tiled=True)  104 us
    all_gather x1, waiting for transfers between devices, local(): left_whole = lax.all_gather(left_env, 'col', axis=1, tiled=True)  44.7 us
    unnamed x23, local copies, waits for them, and re-layouts  35.7 us
    another operation x3, local copies, waits for them, and re-layouts, local(): totals = total(jnp.stack(locals_list))  18.4 us
  transfers between devices with their start and end apart: 8, of which 8 were waited for; matrix products, arithmetic and copies ran while one was open for 5% of the time, Pallas kernels for 0%

commit v1 on v0

--- a/solution.py
+++ b/solution.py
@@ -41,7 +41,10 @@
 
     def apply(stacked):
         panels = stacked.shape[1]
-        whole = lax.all_gather(stacked.astype(jnp.bfloat16), "row", axis=0, tiled=True)
+        frame = stacked.astype(jnp.bfloat16)
+        whole = jnp.concatenate(
+            lax.all_to_all(jnp.stack([frame] * lax.psum(1, "row")), "row", 0, 0), axis=0
+        )
         flat = whole.reshape(whole.shape[0], panels * physical * cols_here)
         left_three = left_whole.reshape(rows_here, flat.shape[0], channels)
         mixed = lax.dot_general(

time: 881 us -> 797 us (0.905)
  waiting for transfers between devices: 388 us -> 238 us
  blocking collectives: 260 us -> 331 us
    all_gather x3 -> x0, waiting for transfers between devices: 104 us -> none  [apply(): lax.all_gather(stacked.astype(jnp.bfloat16), 'row', axis=0, tiled=True)]
    all_to_all x0 -> x2, blocking collectives: none -> 71.5 us  [apply(): lax.all_to_all(jnp.stack([frame] * lax.psum(1, 'row')), 'row', 0, 0)]
    all_gather x1, waiting for transfers between devices: 44.7 us -> 0.02 us  [local(): left_whole = lax.all_gather(left_env, 'col', axis=1, tiled=True)]
    all_to_all x0 -> x1, waiting for transfers between devices: none -> 28 us  [apply(): lax.all_to_all(jnp.stack([frame] * lax.psum(1, 'row')), 'row', 0, 0)]
    unnamed x11 -> x8, waiting for transfers between devices: 225 us -> 210 us
    all_gather x1, waiting for transfers between devices: 14.8 us -> 0.01 us  [local(): right_whole = lax.all_gather(right_env, 'row', axis=0, tiled=True)]
    all_gather x3 -> x0, local copies, waits for them, and re-layouts: 12.3 us -> none  [apply(): lax.all_gather(stacked.astype(jnp.bfloat16), 'row', axis=0, tiled=True)]
    unnamed x23 -> x47, local copies, waits for them, and re-layouts: 35.7 us -> 47.8 us
  transfers between devices with their start and end apart: 8 -> 6, of which waited for: 8 -> 4; matrix products, arithmetic and copies ran while one was open for 5% -> 5% of each run, Pallas kernels for 0% -> 0%
where the time goes in v1:
time: 797 us; the launch traced here: 793 us
  blocking collectives  331 us (42%)
  waiting for transfers between devices  238 us (30%)
  local copies, waits for them, and re-layouts  125 us (16%)
  matrix products  42 us (5%)
  between operations  34.6 us (4%)
  other arithmetic  15.3 us (2%)
    psum x8, blocking collectives, total(): return lax.psum(lax.psum(values, 'col'), 'row')  260 us
    unnamed x8, waiting for transfers between devices  210 us
    all_to_all x2, blocking collectives, apply(): lax.all_to_all(jnp.stack([frame] * lax.psum(1, 'row')), 'row', 0, 0)  71.5 us
    unnamed x47, local copies, waits for them, and re-layouts  47.8 us
    all_to_all x1, waiting for transfers between devices, apply(): lax.all_to_all(jnp.stack([frame] * lax.psum(1, 'row')), 'row', 0, 0)  28 us
    another operation x3, local copies, waits for them, and re-layouts, local(): totals = total(jnp.stack(locals_list))  18.1 us
  transfers between devices with their start and end apart: 6, of which 4 were waited for; matrix products, arithmetic and copies ran while one was open for 5% of the time, Pallas kernels for 0%

profile of v1, /device:TPU:1, one launch (start us, length us, event | category | flops | bytes accessed | tf_op | source)
XLA Modules:
  0.0 792.7 jit_solution(15295464829394072419)
XLA Ops:
  8.6 1.5 fusion.79
  10.2 1.4 pad_maximum_fusion.3
  11.5 34.3 %psum.56 = f32[2]{0:T(128)S(1)} all-reduce(f32[2]{0:T(128)S(1)} %pad_maximum_fusion.3), channel_id=1, replica_groups=mesh['row'=16,'col'=16] {'col'}, use_global_device_ids=true, to_apply=%region_2.0 | all-reduce | flops 2 | bytes 16 | tf_op jit(solution)/shard_map/psum | solution.py:15
  45.8 34.3 %psum.57 = f32[2]{0:T(128)S(1)} all-reduce(f32[2]{0:T(128)S(1)} %psum.56), channel_id=1, replica_groups=mesh['row'=16,'col'=16] {'row'}, use_global_device_ids=true, to_apply=%region_3.0 | all-reduce | flops 2 | bytes 16 | tf_op jit(solution)/shard_map/psum | solution.py:15
  82.0 0.9 fusion.138
  83.9 2.3 reshape.709
  86.2 6.1 all-to-all-start
  93.0 28.0 %all-to-all-done = bf16[16,2,16384]{2,1,0:T(2,128)(2,1)S(1)} async-done(((bf16[16,2,16384]{2,1,0:T(2,128)(2,1)}), bf16[16,2,16384]{2,1,0:T(2,128)(2,1)S(1)}, u32[]{:S(2)}, u32[]{:S(2)}) %all-to-all-start) | async-done | bytes 1048608 | tf_op jit(solution)/shard_map/all_to_all | solution.py:46
  121.0 1.3 reshape.710
  122.3 1.3 reshape.576
  123.6 4.8 copy.49
  128.4 4.5 copy.50
  132.9 2.2 fusion.18
  135.1 4.7 reshape.553
  139.8 3.4 fusion.9
  143.2 4.2 copy.53
  147.4 4.6 fusion.5
  152.0 3.2 copy.101
  155.2 5.6 reshape.703
  160.9 73.8 %reduce-scatter.10.cloned.1.call-done = f32[64,512]{1,0:T(8,128)} async-done(((f32[1024,512]{1,0:T(8,128)}), f32[64,512]{1,0:T(8,128)}) %reduce-scatter.10.cloned.1.call-update) | async-done | bytes 131088
  234.7 1.1 reshape.704
  236.8 4.3 stack.203
  241.1 30.9 %psum.58 = f32[7]{0:T(128)S(1)} all-reduce(f32[7]{0:T(128)S(1)} %stack.203), channel_id=1, replica_groups=mesh['row'=16,'col'=16] {'col'}, use_global_device_ids=true, to_apply=%region_12.0 | all-reduce | flops 7 | bytes 56 | tf_op jit(solution)/shard_map/psum | solution.py:15
  272.0 32.9 %psum.59 = f32[7]{0:T(128)S(1)} all-reduce(f32[7]{0:T(128)S(1)} %psum.58), channel_id=1, replica_groups=mesh['row'=16,'col'=16] {'row'}, use_global_device_ids=true, to_apply=%region_13.0 | all-reduce | flops 7 | bytes 56 | tf_op jit(solution)/shard_map/psum | solution.py:15
  318.5 1.5 reshape.711
  319.9 35.7 %all_to_all.15 = bf16[16,2,16384]{2,1,0:T(2,128)(2,1)} all-to-all(bf16[16,2,16384]{2,1,0:T(2,128)(2,1)S(1)} %reshape.711), channel_id=1, replica_groups=mesh['row'=16,'col'=16] {'row'}, dimensions={0} | all-to-all | bytes 2097152 | tf_op jit(solution)/shard_map/all_to_all | solution.py:46
  355.6 4.5 reshape.712
  360.1 1.3 reshape.581
  361.3 3.8 fusion.19
  365.2 3.6 reshape.559
  368.8 3.1 fusion.12
  371.9 5.8 copy.59
  377.7 4.6 fusion.3
  382.3 3.2 copy.103
  385.5 5.6 reshape.705
  393.7 67.9 %reduce-scatter.12.cloned.1.call-done = f32[64,512]{1,0:T(8,128)} async-done(((f32[1024,512]{1,0:T(8,128)}), f32[64,512]{1,0:T(8,128)}) %reduce-scatter.12.cloned.1.call-update) | async-done | bytes 131088
  461.6 1.1 reshape.706
  463.8 8.1 %stack.221 = f32[13]{0:T(128)S(1)} concatenate(f32[1]{0:T(128)} %bitcast.44, f32[1]{0:T(128)} %bitcast.45, f32[1]{0:T(128)} %bitcast.46, f32[1]{0:T(128)} %bitcast.47, f32[1]{0:T(128)} %bitcast.49, f32[1]{0:T(128)} %bitcast.50, f32[1]{0:T(128)} %bitcast.51, f32[1]{0:T(128)} %bitcast.52, f32[1]{0:T(128)} %bitcast.53, f32[1]{0:T(128)} %bitcast.54, f32[1]{0:T(128)} %bitcast.55, ...), dimensions={0} | concatenate | bytes 104 | tf_op jit(solution)/shard_map/stack | solution.py:91
  471.9 0.9 scatter.66
  472.8 30.9 %psum.60 = f32[13]{0:T(128)S(1)} all-reduce(f32[13]{0:T(128)S(1)} %stack.221), channel_id=1, replica_groups=mesh['row'=16,'col'=16] {'col'}, use_global_device_ids=true, to_apply=%region_28.0 | all-reduce | flops 13 | bytes 104 | tf_op jit(solution)/shard_map/psum | solution.py:15
  503.7 32.9 %psum.61 = f32[13]{0:T(128)S(1)} all-reduce(f32[13]{0:T(128)S(1)} %psum.60), channel_id=1, replica_groups=mesh['row'=16,'col'=16] {'row'}, use_global_device_ids=true, to_apply=%region_29.0 | all-reduce | flops 13 | bytes 104 | tf_op jit(solution)/shard_map/psum | solution.py:15
  538.2 1.5 scatter.70
  541.9 1.8 dynamic-slice.126
  545.5 1.3 scatter.76
  553.0 2.7 subtract_divide_fusion
  557.4 1.5 reshape.713
  558.8 35.8 %all_to_all.16 = bf16[16,2,16384]{2,1,0:T(2,128)(2,1)} all-to-all(bf16[16,2,16384]{2,1,0:T(2,128)(2,1)S(1)} %reshape.713), channel_id=1, replica_groups=mesh['row'=16,'col'=16] {'row'}, dimensions={0} | all-to-all | bytes 2097152 | tf_op jit(solution)/shard_map/all_to_all | solution.py:46
  594.6 4.5 reshape.714
  599.1 1.3 reshape.600
  600.4 3.8 fusion.20
  604.2 3.6 reshape.569
  607.8 3.1 fusion.15
  610.9 5.8 copy.66
  616.7 4.6 fusion.1
  621.3 3.2 copy.105
  624.5 5.6 reshape.707
  631.3 1.3 scatter.64
  632.7 1.3 scatter.85
  634.0 66.6 %reduce-scatter.14.cloned.1.call-done = f32[64,512]{1,0:T(8,128)} async-done(((f32[1024,512]{1,0:T(8,128)}), f32[64,512]{1,0:T(8,128)}) %reduce-scatter.14.cloned.1.call-update) | async-done | bytes 131088
  700.6 1.1 reshape.708
  702.7 5.7 stack.235
  708.6 30.9 %psum.62 = f32[9]{0:T(128)S(1)} all-reduce(f32[9]{0:T(128)S(1)} %stack.235), channel_id=1, replica_groups=mesh['row'=16,'col'=16] {'col'}, use_global_device_ids=true, to_apply=%region_45.0 | all-reduce | flops 9 | bytes 72 | tf_op jit(solution)/shard_map/psum | solution.py:15
  739.6 32.9 %psum.63 = f32[9]{0:T(128)S(1)} all-reduce(f32[9]{0:T(128)S(1)} %psum.62), channel_id=1, replica_groups=mesh['row'=16,'col'=16] {'row'}, use_global_device_ids=true, to_apply=%region_46.0 | all-reduce | flops 9 | bytes 72 | tf_op jit(solution)/shard_map/psum | solution.py:15
  780.5 3.9 multiply_add_fusion
  (136 shorter events, 28.7 us)
Async XLA Ops:
  7.2 116.5 %all-gather.3.cloned.1.call-start = ((), (), s32[]{:S(2)}) async-start(), calls=%async_computation.6 | async-start | bytes 2228224 | tf_op jit(solution)/shard_map/all_gather | solution.py:39
  7.9 139.5 %all-gather.5.cloned.1.call-start = ((), (), s32[]{:S(2)}) async-start(), calls=%async_computation.7 | async-start | bytes 2228224 | tf_op jit(solution)/shard_map/all_gather | solution.py:40
  83.9 8.9 %copy-start.7 = (bf16[16,16,4,4]{1,3,2,0:T(4,128)(2,1)S(1)}, bf16[16,16,4,4]{1,3,2,0:T(4,128)(2,1)}, u32[]{:S(2)}) copy-start(bf16[16,16,4,4]{1,3,2,0:T(4,128)(2,1)} %param.46) | copy-start | bytes 24580
  86.2 34.8 %all-to-all-start = ((bf16[16,2,16384]{2,1,0:T(2,128)(2,1)}), bf16[16,2,16384]{2,1,0:T(2,128)(2,1)S(1)}, u32[]{:S(2)}, u32[]{:S(2)}) async-start(bf16[16,2,16384]{2,1,0:T(2,128)(2,1)} %reshape.709), calls=%async_computation | async-start | bytes 2097152 | tf_op jit(solution)/shard_map/all_to_all | solution.py:46
  92.2 142.5 %reduce-scatter.10.cloned.1.call-start = ((), (), s32[]{:S(2)}) async-start(), calls=%async_computation.8 | async-start | bytes 2228224
  93.0 46.8 %copy-start.8 = (bf16[16,16,4,4,1,1]{0,1,2,3,5,4:T(8,128)(2,1)}, bf16[16,16,4,4,1,1]{0,1,2,3,5,4:T(8,128)(2,1)S(1)}, u32[]{:S(2)}) copy-start(bf16[16,16,4,4,1,1]{0,1,2,3,5,4:T(8,128)(2,1)S(1)} %copy.71) | copy-start | bytes 24580
  132.9 2.2 copy-start.6
  160.8 75.1 %copy-start.11 = (f32[4]{0:T(128)S(1)}, f32[4]{0:T(128)}, u32[]{:S(2)}) copy-start(f32[4]{0:T(128)} %param.47) | copy-start | bytes 52
  160.8 75.2 %copy-start = (bf16[64,4,64]{2,1,0:T(4,128)(2,1)S(1)}, bf16[64,4,64]{2,1,0:T(4,128)(2,1)}, u32[]{:S(2)}) copy-start(bf16[64,4,64]{2,1,0:T(4,128)(2,1)} %param.42) | copy-start | bytes 98308
  160.8 75.2 %copy-start.1 = (bf16[64,4,64]{2,1,0:T(4,128)(2,1)S(1)}, bf16[64,4,64]{2,1,0:T(4,128)(2,1)}, u32[]{:S(2)}) copy-start(bf16[64,4,64]{2,1,0:T(4,128)(2,1)} %param.43) | copy-start | bytes 98308
  160.8 300.8 %reduce-scatter.12.cloned.1.call-start = ((), (), s32[]{:S(2)}) async-start(), calls=%async_computation.9 | async-start | bytes 2228224
  365.2 3.6 copy-start.9
  391.1 309.4 %reduce-scatter.14.cloned.1.call-start = ((), (), s32[]{:S(2)}) async-start(), calls=%async_computation.10 | async-start | bytes 2228224
  555.8 0.7 copy-start.2
  555.8 0.7 copy-start.4
  604.2 3.6 copy-start.10
  630.1 71.7 %copy-start.3 = (f32[64,4,64]{2,0,1:T(8,128)S(1)}, f32[64,4,64]{2,0,1:T(8,128)}, u32[]{:S(2)}) copy-start(f32[64,4,64]{2,0,1:T(8,128)} %copy-done.2) | copy-start | bytes 196612
  630.1 71.7 %copy-start.5 = (f32[64,4,64]{2,0,1:T(8,128)S(1)}, f32[64,4,64]{2,0,1:T(8,128)}, u32[]{:S(2)}) copy-start(f32[64,4,64]{2,0,1:T(8,128)} %copy-done.4) | copy-start | bytes 196612
  630.1 142.6 %copy-start.12 = (f32[3,1]{0,1:T(1,128)S(1)}, f32[3,1]{0,1:T(1,128)}, u32[]{:S(2)}) copy-start(f32[3,1]{0,1:T(1,128)} %constant.468) | copy-start | bytes 40
Sparse Core Ops, SparseCore 0:
  10.5 52.1 all-gather.2
  64.5 49.4 all-gather.4
  161.0 73.7 reduce-scatter.9
  391.3 70.2 reduce-scatter.11
  630.3 70.2 reduce-scatter.13
